TPU v7x, 256 devices: a whole 4x4x8 slice. The times are simulated.
256 devices in a mesh: space: 64 (over z, x, core), head: 4 (over y).
Axes of the slice: x: 4, y: 4, z: 8, core: 2. Of those that a mesh axis runs over, the one named last changes fastest.
Arguments:
- features: bfloat16 [512, 16, 16, 128], P('space', None, None, 'head'), may hold values from -6 to 6
- mask: int32 [512, 16, 16], P('space'), may hold values from 0 to 1, as said below
- conv1_weight: bfloat16 [27, 128, 128], replicated, may hold values from -0.21875 to 0.21875
- conv2_weight: bfloat16 [27, 128, 128], replicated, may hold values from -0.21875 to 0.21875
- down_weight: bfloat16 [8, 128, 512], replicated, may hold values from -0.1875 to 0.1875
- norm_gain: float32 [512], replicated, may hold values from 0.1 to 1.9
- qkv_weight: bfloat16 [512, 3, 512], P(None, None, 'head'), may hold values from -2 to 2
- out_weight: bfloat16 [512, 512], P('head'), may hold values from -0.25 to 0.25
Outputs:
- refined: bfloat16 [512, 16, 16, 128], P('space', None, None, 'head')
- level_out: bfloat16 [16384, 512], P('space', 'head')
Inputs may be any that keep to these rules, and one draw needn't show every extreme that they name: `mask`: A voxel is occupied only inside an active brick of 8^3 aligned voxels; the first brick and its first voxel are always occupied.
All inputs are finite; a program needn't handle non-finite values.
Results may differ from a plain program's by a relative error of at most 0.012.
Values may be sent and summed in bfloat16 or wider, within the bound.
No kernel may reach another device: no remote copies, remote signals or barrier semaphores. Data moves between devices by JAX's collectives and lax.ppermute only.
A program may use at most 64 MiB of HBM per device.

v0:
```python
import jax
import jax.numpy as jnp
from jax import lax
from jax.sharding import PartitionSpec as P

HEADS = 8
KEY_BLOCK = 1024


def with_halo(cells, axis, width):
    count = lax.axis_size(axis)
    ends = count - 1
    head = lax.slice_in_dim(cells, 0, width, axis=0)
    tail = lax.slice_in_dim(cells, cells.shape[0] - width, cells.shape[0], axis=0)
    return jnp.concatenate(
        [
            lax.ppermute(tail, axis, [(i, i + 1) for i in range(ends)]),
            cells,
            lax.ppermute(head, axis, [(i + 1, i) for i in range(ends)]),
        ],
        axis=0,
    )


def convolve(rimmed, weight):
    chans = weight.shape[1]
    kernel = weight.reshape(3, 3, 3, chans, weight.shape[2])
    out = lax.conv_general_dilated(
        rimmed[None],
        kernel,
        window_strides=(1, 1, 1),
        padding=((0, 0), (1, 1), (1, 1)),
        dimension_numbers=("NDHWC", "DHWIO", "NDHWC"),
        preferred_element_type=jnp.float32,
    )
    return out[0]


def to_cells(field):
    nx, ny, nz, count = field.shape
    blocks = field.reshape(nx // 2, 2, ny // 2, 2, nz // 2, 2, count).transpose(0, 2, 4, 1, 3, 5, 6)
    return blocks.reshape(nx // 2 * (ny // 2) * (nz // 2), 8 * count)


def body(
    features, mask, conv1_weight, conv2_weight, down_weight, norm_gain, qkv_weight, out_weight
):
    member = lax.axis_index("head")
    nx, ny, nz, local = features.shape
    width = down_weight.shape[2]
    chans = conv1_weight.shape[1]
    tokens = nx // 2 * (ny // 2) * (nz // 2)
    occupied = mask.astype(jnp.float32)[..., None]
    masked = features * mask.astype(jnp.bfloat16)[..., None]
    rimmed = lax.all_gather(with_halo(masked, "space", 1), "head", axis=3, tiled=True)
    whole_masked = lax.slice_in_dim(rimmed, 1, nx + 1, axis=0)
    pre1 = convolve(rimmed, conv1_weight)
    hidden = (occupied * jax.nn.silu(pre1)).astype(jnp.bfloat16)
    pre2 = convolve(with_halo(hidden, "space", 1), conv2_weight)
    refined_all = (occupied * (whole_masked.astype(jnp.float32) + pre2)).astype(jnp.bfloat16)
    refined = lax.dynamic_slice_in_dim(refined_all, member * local, local, 3)
    coarse = jnp.dot(
        to_cells(refined_all),
        down_weight.reshape(8 * chans, width),
        preferred_element_type=jnp.float32,
    ).astype(jnp.bfloat16)
    wide = coarse.astype(jnp.float32)
    normed = (
        wide * lax.rsqrt(jnp.mean(wide * wide, axis=1, keepdims=True) + 1e-05) * norm_gain
    ).astype(jnp.bfloat16)
    local_cols = qkv_weight.shape[2]
    proj = jnp.dot(
        normed, qkv_weight.reshape(width, 3 * local_cols), preferred_element_type=jnp.float32
    )
    proj = proj.astype(jnp.bfloat16).reshape(tokens, 3, local_cols)
    head_size = width // HEADS
    heads_here = local_cols // head_size
    query = proj[:, 0].reshape(tokens, heads_here, head_size)
    live_cell = (
        mask.reshape(nx // 2, 2, ny // 2, 2, nz // 2, 2)
        .max(axis=(1, 3, 5))
        .reshape(1, -1)
        .astype(jnp.bfloat16)
    )
    span = 2 * local_cols
    live_len = -(-tokens // span) * span
    live_rows = jnp.pad(live_cell, ((0, 0), (0, live_len - tokens))).reshape(-1, span)
    live_count = live_rows.shape[0]
    live_rows = jnp.pad(live_rows, ((0, -(-live_count // 8) * 8 - live_count), (0, 0)))
    piece = jnp.concatenate([proj[:, 1], proj[:, 2]], axis=1)
    piece = jnp.concatenate([piece, live_rows], axis=0)
    rows = piece.shape[0]
    gathered = lax.all_gather(piece[None], "space", axis=0, tiled=True)
    parts = gathered.shape[0]
    count = parts * tokens
    piece_keys = gathered[:, :tokens, :local_cols].reshape(count, heads_here, head_size)
    piece_values = gathered[:, :tokens, local_cols:].reshape(count, heads_here, head_size)
    piece_live = (
        gathered[:, tokens : tokens + live_count].reshape(parts, -1)[:, :tokens].reshape(count)
    )
    bias = jnp.where(piece_live > 0, 0.0, -1e30).astype(jnp.float32)
    scale = head_size ** (-0.5)

    def one_block(carry, block):
        top_old, sums, accum = carry
        block_keys, block_values, block_bias = block
        scores = (
            jnp.einsum("qhd,khd->hqk", query, block_keys, preferred_element_type=jnp.float32)
            * scale
            + block_bias[None, None, :]
        )
        top_new = jnp.maximum(top_old, jnp.max(scores, axis=-1))
        expo = jnp.exp(scores - top_new[..., None])
        factor = jnp.exp(top_old - top_new)
        sums = sums * factor + jnp.sum(expo, axis=-1)
        accum = accum * factor[..., None] + jnp.einsum(
            "hqk,khd->hqd",
            expo.astype(jnp.bfloat16),
            block_values,
            preferred_element_type=jnp.float32,
        )
        return ((top_new, sums, accum), None)

    start_state = (
        jnp.full((heads_here, tokens), -1e30, jnp.float32),
        jnp.zeros((heads_here, tokens), jnp.float32),
        jnp.zeros((heads_here, tokens, head_size), jnp.float32),
    )
    size = KEY_BLOCK if count % KEY_BLOCK == 0 else tokens
    blocks = count // size
    stacked = (
        piece_keys.reshape(blocks, size, heads_here, head_size),
        piece_values.reshape(blocks, size, heads_here, head_size),
        bias.reshape(blocks, size),
    )
    carry, unused = lax.scan(one_block, start_state, stacked)
    top_final, sums, accum = carry
    attn = (
        (accum / sums[..., None])
        .transpose(1, 0, 2)
        .reshape(tokens, local_cols)
        .astype(jnp.bfloat16)
    )
    cols_w = lax.all_to_all(out_weight, "head", 1, 0, tiled=True)
    attn_all = lax.all_gather(attn, "head", axis=1, tiled=True)
    mixed = jnp.dot(attn_all, cols_w, preferred_element_type=jnp.float32)
    mine = lax.dynamic_slice_in_dim(wide, member * local_cols, local_cols, 1)
    level_out = (mine + mixed).astype(jnp.bfloat16)
    return (refined, level_out)


def solution(mesh):
    in_specs = (
        P("space", None, None, "head"),
        P("space", None, None),
        P(),
        P(),
        P(),
        P(),
        P(None, None, "head"),
        P("head", None),
    )
    out_specs = (P("space", None, None, "head"), P("space", "head"))
    return jax.shard_map(body, mesh=mesh, in_specs=in_specs, out_specs=out_specs, check_vma=False)
```

profile of v0, /device:TPU:8, one launch (start us, length us, event | category | flops | bytes accessed | tf_op | source)
XLA Modules:
  0.0 343.7 jit_solution(4440227885603397588)
XLA Ops:
  7.2 1.0 fusion.60
  8.2 2.7 copy.59
  11.1 1.7 collective-permute-start
  12.8 1.3 collective-permute-start.1
  14.2 3.1 collective-permute-done.1
  17.6 45.3 %all_gather.9 = bf16[10,16,16,128]{2,1,0,3:T(8,128)(2,1)} all-gather(bf16[10,16,16,32]{2,1,0,3:T(8,128)(2,1)S(1)} %pad_maximum_fusion), channel_id=1, replica_groups=mesh['space'=64,'head'=4] {'head'}, dimensions={3}, use_global_device_ids=true | all-gather | bytes 819200 | tf_op jit(solution)/shard_map/all_gather | solution.py:55
  62.9 5.2 %copy.60 = bf16[10,16,16,128]{3,1,2,0:T(8,128)(2,1)S(1)} copy(bf16[10,16,16,128]{2,1,0,3:T(8,128)(2,1)} %all_gather.9) | data formatting | bytes 1310720 | tf_op jit(solution)/shard_map/all_gather | solution.py:55
  68.8 0.5 copy-done.5
  69.3 6.2 %fusion.35 = f32[8,16,8,3,128]{4,2,3,1,0:T(8,128)S(1)} fusion(bf16[3,3,3,128,128]{4,3,2,1,0:T(8,128)(2,1)S(1)} %bitcast.110, bf16[10,16,1,7,2,128]{5,3,4,1,0,2:T(8,128)(2,1)S(1)} %slice.51, bf16[10,16,1,8,3,128]{5,3,4,1,0,2:T(8,128)(2,1)S(1)} %copy.63, pred[8,3]{0,1:T(4,128)(4,1)S(1)} %copy-done.7), kind=kOutput, calls=%fused_computation.40 | convolution fusion | flops 2609971200 | bytes 4014104 | tf_op jit(solution)/shard_map/conv_general_dilated | solution.py:28
  76.1 4.3 %collective-permute-start.2 = (bf16[1,16,16,128]{3,1,2,0:T(8,128)(2,1)S(1)}, bf16[1,16,16,128]{3,1,2,0:T(8,128)(2,1)S(1)}, u32[]{:S(2)}, u32[]{:S(2)}) collective-permute-start(bf16[1,16,16,128]{3,1,2,0:T(8,128)(2,1)S(1)} %get-tuple-element.128), channel_id=1, source_target_pairs={{0,4},{4,8},{8,12},{12,16},{16,20},{20,24},{24,28},{28,32},{32,36}... | collective-permute-start | bytes 196616 | tf_op jit(solution)/shard_map/ppermute | solution.py:17
  80.5 1.5 collective-permute-start.3
  82.1 1.2 copy.69
  83.3 0.6 reduce_max.18
  84.1 1.9 collective-permute-done.3
  86.7 0.5 copy-done.6
  87.2 6.2 %fusion.32 = f32[8,16,8,3,128]{4,2,3,1,0:T(8,128)S(1)} fusion(bf16[3,3,3,128,128]{4,3,2,1,0:T(8,128)(2,1)S(1)} %bitcast.111, bf16[10,16,1,7,2,128]{5,3,4,1,0,2:T(8,128)(2,1)S(1)} %slice.55, bf16[10,16,1,8,3,128]{5,3,4,1,0,2:T(8,128)(2,1)S(1)} %copy.66, pred[8,3]{0,1:T(4,128)(4,1)S(1)} %copy-done.7), kind=kOutput, calls=%fused_computation.39 | convolution fusion | flops 2609971200 | bytes 4014104 | tf_op jit(solution)/shard_map/conv_general_dilated | solution.py:28
  94.4 0.5 multiply_reduce_fusion
  95.5 0.8 copy.74
  96.3 0.8 copy.79
  97.1 4.5 %all-to-all-start = ((bf16[128,4,128]{0,2,1:T(8,128)(2,1)}), bf16[128,4,128]{0,2,1:T(8,128)(2,1)S(1)}, u32[]{:S(2)}, u32[]{:S(2)}) async-start(bf16[128,4,128]{0,2,1:T(8,128)(2,1)} %bitcast.24), calls=%async_computation | async-start | bytes 262144 | tf_op jit(solution)/shard_map/all_to_all | solution.py:144
  101.8 0.9 copy.81
  102.7 3.4 all-to-all-done
  106.2 82.1 %all-gather.3.cloned.1.call-done = bf16[16896,256]{1,0:T(8,128)(2,1)} async-done(((bf16[264,256]{1,0:T(8,128)(2,1)}), bf16[16896,256]{1,0:T(8,128)(2,1)}) %all-gather.3.cloned.1.call-update) | async-done | bytes 8650768 | tf_op jit(solution)/shard_map/all_gather | solution.py:93
  188.3 1.1 fusion.49
  189.5 6.0 %fusion.56 = (bf16[64,256,128]{2,1,0:T(8,128)(2,1)}, bf16[64,256,128]{2,1,0:T(8,128)(2,1)}) fusion(bf16[64,264,256]{2,1,0:T(8,128)(2,1)} %bitcast.93), kind=kLoop, calls=%fused_computation.77 | loop fusion | bytes 16777216 | tf_op jit(solution)/shard_map/slice | solution.py:97
  195.5 14.7 %reshape.108 = bf16[16,1024,2,64]{3,2,1,0:T(2,128)(2,1)} reshape(bf16[64,256,128]{2,1,0:T(8,128)(2,1)} %get-tuple-element.124) | data formatting | bytes 8388608 | tf_op jit(solution)/shard_map/reshape;reshape | solution.py:133
  210.2 20.1 %copy.78 = bf16[16,1024,2,64]{1,3,2,0:T(8,128)(2,1)} copy(bf16[16,1024,2,64]{3,2,1,0:T(2,128)(2,1)} %reshape.108) | data formatting | bytes 8388608
  230.3 14.7 %reshape.107 = bf16[16,1024,2,64]{3,2,1,0:T(2,128)(2,1)} reshape(bf16[64,256,128]{2,1,0:T(8,128)(2,1)} %get-tuple-element.125) | data formatting | bytes 8388608 | tf_op jit(solution)/shard_map/reshape;reshape | solution.py:132
  245.0 20.1 %copy.77 = bf16[16,1024,2,64]{1,3,2,0:T(8,128)(2,1)} copy(bf16[16,1024,2,64]{3,2,1,0:T(2,128)(2,1)} %reshape.107) | data formatting | bytes 8388608
  265.1 58.0 %while.15 = (s32[]{:T(128)}, f32[2,256]{1,0:T(2,128)S(1)}, f32[2,256]{1,0:T(2,128)S(1)}, f32[2,256,64]{1,2,0:T(8,128)S(1)}, bf16[16,1024,2,64]{1,3,2,0:T(8,128)(...) while((s32[]{:T(128)}, f32[2,256]{1,0:T(2,128)S(1)}, ...), condition=%wide.region_5.6_spmd.clone, body=%wide.region_2.5_spmd.clone.sunk | while | flops 140085760 | bytes 7196805 | solution.py:136
  265.1 1.5 bitcast_reduce_fusion.2
  267.1 1.6 convolution_add_fusion.3
  268.7 1.5 bitcast_reduce_fusion.2
  270.7 1.6 convolution_add_fusion.3
  272.4 1.5 bitcast_reduce_fusion.2
  274.4 1.6 convolution_add_fusion.3
  276.0 1.5 bitcast_reduce_fusion.2
  278.0 1.6 convolution_add_fusion.3
  279.6 1.5 bitcast_reduce_fusion.2
  281.6 1.6 convolution_add_fusion.3
  283.3 1.5 bitcast_reduce_fusion.2
  285.3 1.6 convolution_add_fusion.3
  286.9 1.5 bitcast_reduce_fusion.2
  288.9 1.6 convolution_add_fusion.3
  290.5 1.5 bitcast_reduce_fusion.2
  292.5 1.6 convolution_add_fusion.3
  294.1 1.5 bitcast_reduce_fusion.2
  296.1 1.6 convolution_add_fusion.3
  297.8 1.5 bitcast_reduce_fusion.2
  299.8 1.6 convolution_add_fusion.3
  301.4 1.5 bitcast_reduce_fusion.2
  303.4 1.6 convolution_add_fusion.3
  305.0 1.5 bitcast_reduce_fusion.2
  307.0 1.6 convolution_add_fusion.3
  308.7 1.5 bitcast_reduce_fusion.2
  310.7 1.6 convolution_add_fusion.3
  312.3 1.5 bitcast_reduce_fusion.2
  314.3 1.6 convolution_add_fusion.3
  315.9 1.5 bitcast_reduce_fusion.2
  317.9 1.6 convolution_add_fusion.3
  319.5 1.5 bitcast_reduce_fusion.2
  321.6 1.6 convolution_add_fusion.3
  323.2 12.8 %all_gather.11 = bf16[256,512]{0,1:T(8,128)(2,1)S(1)} all-gather(bf16[256,128]{0,1:T(8,128)(2,1)S(1)} %bitcast.109), channel_id=1, replica_groups=mesh['space'=64,'head'=4] {'head'}, dimensions={1}, use_global_device_ids=true | all-gather | bytes 327680 | tf_op jit(solution)/shard_map/all_gather | solution.py:145
  336.0 0.9 fusion.39
  (130 shorter events, 13.2 us)
Async XLA Ops:
  7.2 87.3 %copy-start = (bf16[8,128,512]{2,1,0:T(8,128)(2,1)S(1)}, bf16[8,128,512]{2,1,0:T(8,128)(2,1)}, u32[]{:S(2)}) copy-start(bf16[8,128,512]{2,1,0:T(8,128)(2,1)} %param.14) | copy-start | bytes 3145732
  7.2 181.2 %all-gather.3.cloned.1.call-start = ((), (), s32[]{:S(2)}) async-start(), calls=%async_computation.1 | async-start | bytes 8785920 | tf_op jit(solution)/shard_map/all_gather | solution.py:93
  11.1 3.1 collective-permute-start
  12.8 4.5 %collective-permute-start.1 = (bf16[1,16,16,32]{2,1,0,3:T(8,128)(2,1)S(1)}, bf16[1,16,16,32]{2,1,0,3:T(8,128)(2,1)S(1)}, u32[]{:S(2)}, u32[]{:S(2)}) collective-permute-start(bf16[1,16,16,32]{2,1,0,3:T(8,128)(2,1)S(1)} %get-tuple-element.127), channel_id=1, source_target_pairs={{4,0},{8,4},{12,8},{16,12},{20,16},{24,20},{28,24},{32,28},{36,32}... | collective-permute-start | bytes 49160 | tf_op jit(solution)/shard_map/ppermute | solution.py:19
  68.1 1.2 copy-start.5
  68.1 1.2 copy-start.7
  75.5 6.5 %copy-start.2 = (s32[8,16,16]{2,1,0:T(8,128)S(1)}, s32[8,16,16]{2,1,0:T(8,128)}, u32[]{:S(2)}) copy-start(s32[8,16,16]{2,1,0:T(8,128)} %param.11) | copy-start | bytes 24580
  76.1 7.9 %collective-permute-start.2 = (bf16[1,16,16,128]{3,1,2,0:T(8,128)(2,1)S(1)}, bf16[1,16,16,128]{3,1,2,0:T(8,128)(2,1)S(1)}, u32[]{:S(2)}, u32[]{:S(2)}) collective-permute-start(bf16[1,16,16,128]{3,1,2,0:T(8,128)(2,1)S(1)} %get-tuple-element.128), channel_id=1, source_target_pairs={{0,4},{4,8},{8,12},{12,16},{16,20},{20,24},{24,28},{28,32},{32,36}... | collective-permute-start | bytes 196616 | tf_op jit(solution)/shard_map/ppermute | solution.py:17
  80.5 5.5 %collective-permute-start.3 = (bf16[1,16,16,128]{3,1,2,0:T(8,128)(2,1)S(1)}, bf16[1,16,16,128]{3,1,2,0:T(8,128)(2,1)S(1)}, u32[]{:S(2)}, u32[]{:S(2)}) collective-permute-start(bf16[1,16,16,128]{3,1,2,0:T(8,128)(2,1)S(1)} %get-tuple-element.129), channel_id=1, source_target_pairs={{4,0},{8,4},{12,8},{16,12},{20,16},{24,20},{28,24},{32,28},{36,32}... | collective-permute-start | bytes 196616 | tf_op jit(solution)/shard_map/ppermute | solution.py:19
  86.0 1.2 copy-start.6
  94.1 0.9 copy-start.4
  94.4 1.9 copy-start.3
  97.1 9.0 %all-to-all-start = ((bf16[128,4,128]{0,2,1:T(8,128)(2,1)}), bf16[128,4,128]{0,2,1:T(8,128)(2,1)S(1)}, u32[]{:S(2)}, u32[]{:S(2)}) async-start(bf16[128,4,128]{0,2,1:T(8,128)(2,1)} %bitcast.24), calls=%async_computation | async-start | bytes 262144 | tf_op jit(solution)/shard_map/all_to_all | solution.py:144
  323.1 13.7 %copy-start.1 = (bf16[8,128,512]{2,1,0:T(8,128)(2,1)S(1)}, bf16[8,128,512]{2,1,0:T(8,128)(2,1)}, u32[]{:S(2)}) copy-start(bf16[8,128,512]{2,1,0:T(8,128)(2,1)} %param.14) | copy-start | bytes 3145732
Sparse Core Ops, SparseCore 0:
  96.4 91.8 all-gather.2
where the time goes:
time: 347 us; the launch traced here: 344 us
  local copies, waits for them, and re-layouts  91.5 us (26%)
  waiting for transfers between devices  90.5 us (26%)
  matrix products  62.8 us (18%)
  blocking collectives  58.1 us (17%)
  between operations  14.4 us (4%)
  starting transfers between devices  13.4 us (4%)
  other arithmetic  12.2 us (4%)
    all_gather x1, waiting for transfers between devices, body(): gathered = lax.all_gather(piece[None], 'space', axis=0, tiled=True)  82.1 us
    unnamed x22, local copies, waits for them, and re-layouts  46.9 us
    all_gather x1, blocking collectives, body(): lax.all_gather(with_halo(masked, 'space', 1), 'head', axis=3, tiled=True)  45.3 us
    dot_general x16, matrix products, one_block(): jnp.einsum('hqk,khd->hqd', expo.astype(jnp.bfloat16), block_values, prefe...  25.1 us
    dot_general x16, matrix products, one_block(): jnp.einsum('qhd,khd->hqk', query, block_keys, preferred_element_type=jnp....  23.6 us
    another operation x1, local copies, waits for them, and re-layouts, body(): piece_values.reshape(blocks, size, heads_here, head_size)  14.7 us
    another operation x1, local copies, waits for them, and re-layouts, body(): piece_keys.reshape(blocks, size, heads_here, head_size)  14.7 us
    all_gather x1, blocking collectives, body(): attn_all = lax.all_gather(attn, 'head', axis=1, tiled=True)  12.8 us
  transfers between devices with their start and end apart: 6, of which 4 were waited for; matrix products, arithmetic and copies ran while one was open for 1% of the time, Pallas kernels for 0%

commit v1 on v0

--- a/solution.py
+++ b/solution.py
@@ -90,7 +90,9 @@
     piece = jnp.concatenate([proj[:, 1], proj[:, 2]], axis=1)
     piece = jnp.concatenate([piece, live_rows], axis=0)
     rows = piece.shape[0]
-    gathered = lax.all_gather(piece[None], "space", axis=0, tiled=True)
+    gathered = jnp.concatenate(
+        lax.all_to_all(jnp.stack([piece[None]] * lax.axis_size("space")), "space", 0, 0), axis=0
+    )
     parts = gathered.shape[0]
     count = parts * tokens
     piece_keys = gathered[:, :tokens, :local_cols].reshape(count, heads_here, head_size)

time: 347 us -> 459 us (1.32)
  waiting for transfers between devices: 90.5 us -> 193 us
  starting transfers between devices: 13.4 us -> 31.5 us
  between operations: 14.4 us -> 1.08 us
    all_to_all x0 -> x1, waiting for transfers between devices: none -> 190 us  [body(): lax.all_to_all(jnp.stack([piece[None]] * lax.axis_size('space')), 'space'...]
    all_gather x1 -> x0, waiting for transfers between devices: 82.1 us -> none  [body(): gathered = lax.all_gather(piece[None], 'space', axis=0, tiled=True)]
    all_to_all x0 -> x1, starting transfers between devices: none -> 18.4 us  [body(): lax.all_to_all(jnp.stack([piece[None]] * lax.axis_size('space')), 'space'...]
    unnamed x22 -> x24, local copies, waits for them, and re-layouts: 46.9 us -> 46.9 us
  transfers between devices with their start and end apart: 6 -> 6, of which waited for: 4 -> 2; matrix products, arithmetic and copies ran while one was open for 1% -> 3% of each run, Pallas kernels for 0% -> 0%
where the time goes in v1:
time: 459 us; the launch traced here: 455 us
  waiting for transfers between devices  193 us (42%)
  local copies, waits for them, and re-layouts  95.5 us (21%)
  matrix products  62.8 us (14%)
  blocking collectives  57.7 us (13%)
  starting transfers between devices  31.5 us (7%)
  other arithmetic  12.2 us (3%)
    all_to_all x1, waiting for transfers between devices, body(): lax.all_to_all(jnp.stack([piece[None]] * lax.axis_size('space')), 'space'...  190 us
    unnamed x24, local copies, waits for them, and re-layouts  46.9 us
    all_gather x1, blocking collectives, body(): lax.all_gather(with_halo(masked, 'space', 1), 'head', axis=3, tiled=True)  45.3 us
    dot_general x16, matrix products, one_block(): jnp.einsum('hqk,khd->hqd', expo.astype(jnp.bfloat16), block_values, prefe...  25.1 us
    dot_general x16, matrix products, one_block(): jnp.einsum('qhd,khd->hqk', query, block_keys, preferred_element_type=jnp....  23.6 us
    all_to_all x1, starting transfers between devices, body(): lax.all_to_all(jnp.stack([piece[None]] * lax.axis_size('space')), 'space'...  18.4 us
    another operation x1, local copies, waits for them, and re-layouts, body(): piece_values.reshape(blocks, size, heads_here, head_size)  14.8 us
    another operation x1, local copies, waits for them, and re-layouts, body(): piece_keys.reshape(blocks, size, heads_here, head_size)  14.7 us
  transfers between devices with their start and end apart: 6, of which 2 were waited for; matrix products, arithmetic and copies ran while one was open for 3% of the time, Pallas kernels for 0%

profile of v1, /device:TPU:8, one launch (start us, length us, event | category | flops | bytes accessed | tf_op | source)
XLA Modules:
  0.0 455.0 jit_solution(8242564175500330522)
XLA Ops:
  0.6 1.0 fusion.60
  1.6 2.7 copy.56
  4.5 1.7 collective-permute-start
  6.2 1.3 collective-permute-start.1
  7.6 3.1 collective-permute-done.1
  11.0 45.3 %all_gather.6 = bf16[10,16,16,128]{2,1,0,3:T(8,128)(2,1)} all-gather(bf16[10,16,16,32]{2,1,0,3:T(8,128)(2,1)S(1)} %pad_maximum_fusion), channel_id=1, replica_groups=mesh['space'=64,'head'=4] {'head'}, dimensions={3}, use_global_device_ids=true | all-gather | bytes 819200 | tf_op jit(solution)/shard_map/all_gather | solution.py:55
  56.4 5.2 %copy.57 = bf16[10,16,16,128]{3,1,2,0:T(8,128)(2,1)S(1)} copy(bf16[10,16,16,128]{2,1,0,3:T(8,128)(2,1)} %all_gather.6) | data formatting | bytes 1310720 | tf_op jit(solution)/shard_map/all_gather | solution.py:55
  62.2 0.5 copy-done.5
  62.7 6.2 %fusion.35 = f32[8,16,8,3,128]{4,2,3,1,0:T(8,128)S(1)} fusion(bf16[3,3,3,128,128]{4,3,2,1,0:T(8,128)(2,1)S(1)} %bitcast.108, bf16[10,16,1,7,2,128]{5,3,4,1,0,2:T(8,128)(2,1)S(1)} %slice.51, bf16[10,16,1,8,3,128]{5,3,4,1,0,2:T(8,128)(2,1)S(1)} %copy.60, pred[8,3]{0,1:T(4,128)(4,1)S(1)} %copy-done.7), kind=kOutput, calls=%fused_computation.40 | convolution fusion | flops 2609971200 | bytes 4014104 | tf_op jit(solution)/shard_map/conv_general_dilated | solution.py:28
  69.6 0.6 fusion.58
  70.2 4.3 collective-permute-start.2
  74.5 1.3 collective-permute-start.3
  75.8 0.8 copy.76
  76.6 4.5 all-to-all-start.1
  81.3 1.2 copy.66
  82.4 0.6 reduce_max.18
  84.0 0.5 copy-done.6
  84.5 6.2 %fusion.32 = f32[8,16,8,3,128]{4,2,3,1,0:T(8,128)S(1)} fusion(bf16[3,3,3,128,128]{4,3,2,1,0:T(8,128)(2,1)S(1)} %bitcast.109, bf16[10,16,1,7,2,128]{5,3,4,1,0,2:T(8,128)(2,1)S(1)} %slice.55, bf16[10,16,1,8,3,128]{5,3,4,1,0,2:T(8,128)(2,1)S(1)} %copy.63, pred[8,3]{0,1:T(4,128)(4,1)S(1)} %copy-done.8), kind=kOutput, calls=%fused_computation.39 | convolution fusion | flops 2609971200 | bytes 4014104 | tf_op jit(solution)/shard_map/conv_general_dilated | solution.py:28
  91.7 0.5 multiply_reduce_fusion
  92.9 3.9 stack.3
  96.8 18.4 %all-to-all-start = ((bf16[64,1,264,256]{3,2,1,0:T(8,128)(2,1)}), bf16[64,1,264,256]{3,2,1,0:T(8,128)(2,1)}, u32[]{:S(2)}, u32[]{:S(2)}) async-start(bf16[64,1,264,256]{3,2,1,0:T(8,128)(2,1)} %stack.3), calls=%async_computation | async-start | bytes 17301504 | tf_op jit(solution)/shard_map/all_to_all | solution.py:94
  115.4 0.9 copy.78
  116.5 190.3 %all-to-all-done = bf16[64,1,264,256]{3,2,1,0:T(8,128)(2,1)} async-done(((bf16[64,1,264,256]{3,2,1,0:T(8,128)(2,1)}), bf16[64,1,264,256]{3,2,1,0:T(8,128)(2,1)}, u32[]{:S(2)}, u32[]{:S(2)}) %all-to-all-start) | async-done | bytes 8650784 | tf_op jit(solution)/shard_map/all_to_all | solution.py:94
  306.8 1.1 fusion.49
  307.9 6.0 %fusion.56 = (bf16[64,256,128]{2,1,0:T(8,128)(2,1)}, bf16[64,256,128]{2,1,0:T(8,128)(2,1)}) fusion(bf16[64,264,256]{2,1,0:T(8,128)(2,1)} %bitcast.20), kind=kLoop, calls=%fused_computation.77 | loop fusion | bytes 16777216 | tf_op jit(solution)/shard_map/slice | solution.py:99
  313.9 14.8 %reshape.113 = bf16[16,1024,2,64]{3,2,1,0:T(2,128)(2,1)} reshape(bf16[64,256,128]{2,1,0:T(8,128)(2,1)} %get-tuple-element.124) | data formatting | bytes 8388608 | tf_op jit(solution)/shard_map/reshape;reshape | solution.py:135
  328.7 20.1 %copy.75 = bf16[16,1024,2,64]{1,3,2,0:T(8,128)(2,1)} copy(bf16[16,1024,2,64]{3,2,1,0:T(2,128)(2,1)} %reshape.113) | data formatting | bytes 8388608
  348.8 14.7 %reshape.112 = bf16[16,1024,2,64]{3,2,1,0:T(2,128)(2,1)} reshape(bf16[64,256,128]{2,1,0:T(8,128)(2,1)} %get-tuple-element.125) | data formatting | bytes 8388608 | tf_op jit(solution)/shard_map/reshape;reshape | solution.py:134
  363.6 20.1 %copy.74 = bf16[16,1024,2,64]{1,3,2,0:T(8,128)(2,1)} copy(bf16[16,1024,2,64]{3,2,1,0:T(2,128)(2,1)} %reshape.112) | data formatting | bytes 8388608
  383.7 58.0 %while.15 = (s32[]{:T(128)}, f32[2,256]{1,0:T(2,128)S(1)}, f32[2,256]{1,0:T(2,128)S(1)}, f32[2,256,64]{1,2,0:T(8,128)S(1)}, bf16[16,1024,2,64]{1,3,2,0:T(8,128)(...) while((s32[]{:T(128)}, f32[2,256]{1,0:T(2,128)S(1)}, ...), condition=%wide.region_5.6_spmd.clone, body=%wide.region_2.5_spmd.clone.sunk | while | flops 140085760 | bytes 7196805 | solution.py:138
  383.7 1.5 bitcast_reduce_fusion.2
  385.7 1.6 convolution_add_fusion.3
  387.3 1.5 bitcast_reduce_fusion.2
  389.3 1.6 convolution_add_fusion.3
  390.9 1.5 bitcast_reduce_fusion.2
  392.9 1.6 convolution_add_fusion.3
  394.5 1.5 bitcast_reduce_fusion.2
  396.6 1.6 convolution_add_fusion.3
  398.2 1.5 bitcast_reduce_fusion.2
  400.2 1.6 convolution_add_fusion.3
  401.8 1.5 bitcast_reduce_fusion.2
  403.8 1.6 convolution_add_fusion.3
  405.4 1.5 bitcast_reduce_fusion.2
  407.4 1.6 convolution_add_fusion.3
  409.1 1.5 bitcast_reduce_fusion.2
  411.1 1.6 convolution_add_fusion.3
  412.7 1.5 bitcast_reduce_fusion.2
  414.7 1.6 convolution_add_fusion.3
  416.3 1.5 bitcast_reduce_fusion.2
  418.3 1.6 convolution_add_fusion.3
  420.0 1.5 bitcast_reduce_fusion.2
  422.0 1.6 convolution_add_fusion.3
  423.6 1.5 bitcast_reduce_fusion.2
  425.6 1.6 convolution_add_fusion.3
  427.2 1.5 bitcast_reduce_fusion.2
  429.2 1.6 convolution_add_fusion.3
  430.8 1.5 bitcast_reduce_fusion.2
  432.8 1.6 convolution_add_fusion.3
  434.5 1.5 bitcast_reduce_fusion.2
  436.5 1.6 convolution_add_fusion.3
  438.1 1.5 bitcast_reduce_fusion.2
  440.1 1.6 convolution_add_fusion.3
  441.7 12.4 %all_gather.7 = bf16[256,512]{0,1:T(8,128)(2,1)S(1)} all-gather(bf16[256,128]{0,1:T(8,128)(2,1)S(1)} %bitcast.107), channel_id=1, replica_groups=mesh['space'=64,'head'=4] {'head'}, dimensions={1}, use_global_device_ids=true | all-gather | bytes 327680 | tf_op jit(solution)/shard_map/all_gather | solution.py:147
  454.1 0.9 fusion.39
  (132 shorter events, 13.3 us)
Async XLA Ops:
  0.6 91.1 %copy-start = (bf16[8,128,512]{2,1,0:T(8,128)(2,1)S(1)}, bf16[8,128,512]{2,1,0:T(8,128)(2,1)}, u32[]{:S(2)}) copy-start(bf16[8,128,512]{2,1,0:T(8,128)(2,1)} %param.14) | copy-start | bytes 3145732
  4.5 3.1 collective-permute-start
  6.2 4.5 collective-permute-start.1
  61.5 1.2 copy-start.5
  61.6 1.2 copy-start.7
  68.9 6.9 %copy-start.3 = (bf16[128,512]{1,0:T(8,128)(2,1)S(1)}, bf16[128,512]{1,0:T(8,128)(2,1)}, u32[]{:S(2)}) copy-start(bf16[128,512]{1,0:T(8,128)(2,1)} %param.17) | copy-start | bytes 393220
  68.9 12.2 %copy-start.2 = (s32[8,16,16]{2,1,0:T(8,128)S(1)}, s32[8,16,16]{2,1,0:T(8,128)}, u32[]{:S(2)}) copy-start(s32[8,16,16]{2,1,0:T(8,128)} %param.11) | copy-start | bytes 24580
  70.2 13.0 %collective-permute-start.2 = (bf16[1,16,16,128]{3,1,2,0:T(8,128)(2,1)}, bf16[1,16,16,128]{3,1,2,0:T(8,128)(2,1)S(1)}, u32[]{:S(2)}, u32[]{:S(2)}) collective-permute-start(bf16[1,16,16,128]{3,1,2,0:T(8,128)(2,1)} %get-tuple-element.128), channel_id=1, source_target_pairs={{0,4},{4,8},{8,12},{12,16},{16,20},{20,24},{24,28},{28,32},{32,36}... | collective-permute-start | bytes 196616 | tf_op jit(solution)/shard_map/ppermute | solution.py:17
  74.5 8.7 %collective-permute-start.3 = (bf16[1,16,16,128]{3,1,2,0:T(8,128)(2,1)S(1)}, bf16[1,16,16,128]{3,1,2,0:T(8,128)(2,1)S(1)}, u32[]{:S(2)}, u32[]{:S(2)}) collective-permute-start(bf16[1,16,16,128]{3,1,2,0:T(8,128)(2,1)S(1)} %get-tuple-element.129), channel_id=1, source_target_pairs={{4,0},{8,4},{12,8},{16,12},{20,16},{24,20},{28,24},{32,28},{36,32}... | collective-permute-start | bytes 196616 | tf_op jit(solution)/shard_map/ppermute | solution.py:19
  76.6 16.3 %all-to-all-start.1 = ((bf16[128,4,128]{0,2,1:T(8,128)(2,1)}), bf16[128,4,128]{0,2,1:T(8,128)(2,1)S(1)}, u32[]{:S(2)}, u32[]{:S(2)}) async-start(bf16[128,4,128]{0,2,1:T(8,128)(2,1)} %bitcast.24), calls=%async_computation.1 | async-start | bytes 262144 | tf_op jit(solution)/shard_map/all_to_all | solution.py:146
  83.3 1.2 copy-start.6
  83.3 1.2 copy-start.8
  91.3 0.9 copy-start.4
  96.8 210.0 %all-to-all-start = ((bf16[64,1,264,256]{3,2,1,0:T(8,128)(2,1)}), bf16[64,1,264,256]{3,2,1,0:T(8,128)(2,1)}, u32[]{:S(2)}, u32[]{:S(2)}) async-start(bf16[64,1,264,256]{3,2,1,0:T(8,128)(2,1)} %stack.3), calls=%async_computation | async-start | bytes 17301504 | tf_op jit(solution)/shard_map/all_to_all | solution.py:94
  441.7 13.3 %copy-start.1 = (bf16[8,128,512]{2,1,0:T(8,128)(2,1)S(1)}, bf16[8,128,512]{2,1,0:T(8,128)(2,1)}, u32[]{:S(2)}) copy-start(bf16[8,128,512]{2,1,0:T(8,128)(2,1)} %param.14) | copy-start | bytes 3145732
